TPU v7x, 256 devices: a whole 4x4x8 slice. The times are simulated.
256 devices in a mesh: stream: 8 (over z), span: 32 (over y, x, core).
Axes of the slice: x: 4, y: 4, z: 8, core: 2. Of those that a mesh axis runs over, the one named last changes fastest.
Arguments:
- velocity: float32 [3, 64, 512, 1024], P(None, 'stream', 'span'), may hold values from -36 to 36
- coefficient: float32 [64, 512, 1024], P('stream', 'span'), may hold values from 0.5 to 4
- coords: float32 [3, 32768], P(None, ('stream', 'span')), may hold values from -1 to 1
- forces: float32 [3, 32768], P(None, ('stream', 'span')), may hold values from -12 to 12
- line_id: int32 [32768], P(('stream', 'span')), may hold values from 0 to 399
- line_gain: float32 [400], replicated, may hold values from 0.5 to 2
- dest_span: int32 [32768, 1], P(('stream', 'span')), may hold values from 0 to 31; in each aligned block of 128 rows (0 to 127, 128 to 255, ...) at most 8 rows name the same one
- owner_element: int32 [32768], P(('stream', 'span')), may hold values from 0 to 255
Outputs:
- pressure: float32 [64, 512, 1024], P('stream', 'span')
- residual: float32 [64, 512, 1024], P('stream', 'span')
Inputs may be any that keep to these rules, and one draw needn't show every extreme that they name: `dest_span`: of the 128 blade points of one device, at most 8 name the same span index, and in every draw some span index is named by exactly 8 of one device's points. `owner_element`: an element of the device at the point's span index in the same slab, numbered (ex * 2 + ey) * 128 + ez.
All inputs are finite; a program needn't handle non-finite values.
Results may differ from a plain program's by a relative error of at most 0.00019.
Values sent between devices are 32-bit elements; how exact they have to be, the bound alone decides.
No kernel may reach another device: no remote copies, remote signals or barrier semaphores. Data moves between devices by JAX's collectives and lax.ppermute only.
A program may use at most 64 MiB of HBM per device.

v0:
```python
import jax
import jax.numpy as jnp
from jax import lax
from jax.sharding import PartitionSpec as P

POLY = 8
ITERS = 3
kernel_width = 0.45
gll_nodes = [
    -1.0,
    -0.8717401485096066,
    -0.5917001814331423,
    -0.2092992179024789,
    0.2092992179024789,
    0.5917001814331423,
    0.8717401485096066,
    1.0,
]


def with_halo(x, sides, width):
    for axis, dim in sides:
        size, length = (lax.axis_size(axis), x.shape[dim])
        up = [(i, (i + 1) % size) for i in range(size - 1)]
        down = [(j, i) for i, j in up]
        last = lax.slice_in_dim(x, length - width, length, axis=dim)
        first = lax.slice_in_dim(x, 0, width, axis=dim)
        before = lax.ppermute(last, axis, up)
        after = lax.ppermute(first, axis, down)
        x = jnp.concatenate([before, x, after], axis=dim)
    return x


def legendre_value(point, degree):
    previous = 1.0
    current = point
    for order in range(1, degree):
        following = ((2 * order + 1) * point * current - order * previous) / (order + 1)
        previous = current
        current = following
    return current


def gll_tables():
    degree = POLY - 1
    values = [legendre_value(point, degree) for point in gll_nodes]
    weights = [2.0 / (degree * (degree + 1) * value * value) for value in values]
    diffmat = []
    for row_at in range(POLY):
        row_list = []
        for col_at in range(POLY):
            if row_at != col_at:
                row_list.append(
                    values[row_at] / (values[col_at] * (gll_nodes[row_at] - gll_nodes[col_at]))
                )
            elif row_at == 0:
                row_list.append(-degree * (degree + 1) / 4.0)
            elif row_at == degree:
                row_list.append(degree * (degree + 1) / 4.0)
            else:
                row_list.append(0.0)
        diffmat.append(row_list)
    return (
        jnp.asarray(gll_nodes, dtype=jnp.float32),
        jnp.asarray(weights, dtype=jnp.float32),
        jnp.asarray(diffmat, dtype=jnp.float32),
    )


def derive(grid_field, diffmat, axis_at, flipped):
    matrix = diffmat.T if flipped else diffmat
    extent0, extent1, extent2 = grid_field.shape
    highest = lax.Precision.HIGHEST
    if axis_at == 0:
        blocks = grid_field.reshape(extent0 // POLY, POLY, extent1, extent2)
        result = jnp.einsum("ia,xayz->xiyz", matrix, blocks, precision=highest)
    elif axis_at == 1:
        blocks = grid_field.reshape(extent0, extent1 // POLY, POLY, extent2)
        result = jnp.einsum("ib,xybz->xyiz", matrix, blocks, precision=highest)
    else:
        block_width = 128
        tiled_matrix = jnp.kron(jnp.eye(block_width // POLY, dtype=jnp.float32), matrix)
        blocks = grid_field.reshape(extent0, extent1, extent2 // block_width, block_width)
        result = jnp.einsum("xyzc,ic->xyzi", blocks, tiled_matrix, precision=highest)
    return result.reshape(grid_field.shape)


def face_masks(extent):
    node = lax.iota(jnp.int32, extent) % POLY
    return (node == 0, node == POLY - 1)


def assemble(grid_field):
    extent0, extent1, extent2 = grid_field.shape
    first0, last0 = face_masks(extent0)
    first1, last1 = face_masks(extent1)
    first2, last2 = face_masks(extent2)
    first0, last0 = (first0[:, None, None], last0[:, None, None])
    first1, last1 = (first1[None, :, None], last1[None, :, None])
    first2, last2 = (first2[None, None, :], last2[None, None, :])
    nothing = jnp.zeros_like(grid_field)
    padded = with_halo(grid_field, (("stream", 0),), 1)
    running = (
        grid_field + jnp.where(first0, padded[:-2], nothing) + jnp.where(last0, padded[2:], nothing)
    )
    padded = with_halo(running, (("span", 1),), 1)
    running = (
        running
        + jnp.where(first1, padded[:, :-2], nothing)
        + jnp.where(last1, padded[:, 2:], nothing)
    )
    before = jnp.pad(running, ((0, 0), (0, 0), (1, 0)))[:, :, :-1]
    after = jnp.pad(running, ((0, 0), (0, 0), (0, 1)))[:, :, 1:]
    return running + jnp.where(first2, before, nothing) + jnp.where(last2, after, nothing)


def inverse_multiplicity(extent, offset, whole):
    node = lax.iota(jnp.int32, extent) % POLY
    position = offset + lax.iota(jnp.int32, extent)
    inner_face = (node == 0) & (position > 0) | (node == POLY - 1) & (position < whole - 1)
    return jnp.where(inner_face, 0.5, 1.0).astype(jnp.float32)


def apply_operator(grid_field, weight3, metric, diffmat):
    running = weight3 * grid_field
    for axis_at in range(3):
        running = running + derive(
            metric * derive(grid_field, diffmat, axis_at, False), diffmat, axis_at, True
        )
    return assemble(running)


def spread_points(arrived, abscissa, extent0, extent1, extent2):
    slots = arrived.shape[0]
    elems_x, elems_y, elems_z = (extent0 // POLY, extent1 // POLY, extent2 // POLY)
    kernels = []
    for dimension in range(3):
        kernels.append(
            jnp.exp(
                -(((abscissa[None, :] - arrived[:, dimension : dimension + 1]) / kernel_width) ** 2)
            )
        )
    kernel3 = (
        kernels[0][:, :, None, None] * kernels[1][:, None, :, None] * kernels[2][:, None, None, :]
    )
    contrib = (arrived[:, 3:6][:, :, None, None, None] * kernel3[:, None]).reshape(
        slots, 3 * POLY**3
    )
    element_codes = lax.iota(jnp.float32, elems_x * elems_y * elems_z) + 1.0
    onehot = (arrived[:, 6][:, None] == element_codes[None, :]).astype(jnp.float32)
    per_elem = jnp.dot(
        onehot.T, contrib, precision=lax.Precision.HIGHEST, preferred_element_type=jnp.float32
    )
    per_elem = per_elem.reshape(elems_x, elems_y, elems_z, 3, POLY, POLY, POLY)
    return per_elem.transpose(3, 0, 4, 1, 5, 2, 6).reshape(3, extent0, extent1, extent2)


def project_points(coords, forces, line_id, line_gain, dest_span, owner_element, abscissa, extents):
    points_dev = coords.shape[1]
    spans = lax.axis_size("span")
    capacity = max(2, 2 * points_dev // spans)
    table_ids = lax.iota(jnp.int32, line_gain.shape[0])
    gains = jnp.sum(
        jnp.where(line_id[:, None] == table_ids[None, :], line_gain[None, :], 0.0), axis=1
    )
    scaled = forces * gains[None, :]
    target = dest_span[:, 0]
    owner_code = (owner_element + 1).astype(jnp.float32)
    payload = jnp.concatenate(
        [coords, scaled, owner_code[None, :], target.astype(jnp.float32)[None, :]], axis=0
    ).T
    onehot_dest = (target[:, None] == lax.iota(jnp.int32, spans)[None, :]).astype(jnp.int32)
    ranks = jnp.sum((jnp.cumsum(onehot_dest, axis=0) - 1) * onehot_dest, axis=1)
    slot_at = target * capacity + ranks
    outgoing = jnp.zeros((spans * capacity, 8), jnp.float32).at[slot_at].set(payload)
    outgoing = outgoing.reshape(spans, capacity, 8)
    arrived = lax.all_to_all(outgoing, "span", split_axis=0, concat_axis=0, tiled=True).reshape(
        spans * capacity, 8
    )
    return spread_points(arrived, abscissa, extents[0], extents[1], extents[2])


def on_device(velocity, coefficient, coords, forces, line_id, line_gain, dest_span, owner_element):
    abscissa, weights, diffmat = gll_tables()
    extent0, extent1, extent2 = coefficient.shape
    tile_zero = jnp.tile(weights, extent0 // POLY)
    tile_one = jnp.tile(weights, extent1 // POLY)
    tile_two = jnp.tile(weights, extent2 // POLY)
    weight3 = tile_zero[:, None, None] * tile_one[None, :, None] * tile_two[None, None, :]
    metric = weight3 * coefficient
    inv_zero = inverse_multiplicity(
        extent0, lax.axis_index("stream") * extent0, extent0 * lax.axis_size("stream")
    )
    inv_one = inverse_multiplicity(
        extent1, lax.axis_index("span") * extent1, extent1 * lax.axis_size("span")
    )
    inv_two = inverse_multiplicity(extent2, 0, extent2)
    inv_mult = inv_zero[:, None, None] * inv_one[None, :, None] * inv_two[None, None, :]
    forcing = project_points(
        coords,
        forces,
        line_id,
        line_gain,
        dest_span,
        owner_element,
        abscissa,
        (extent0, extent1, extent2),
    )
    running = derive(weight3 * (velocity[0] + forcing[0]), diffmat, 0, True)
    running = running + derive(weight3 * (velocity[1] + forcing[1]), diffmat, 1, True)
    running = running + derive(weight3 * (velocity[2] + forcing[2]), diffmat, 2, True)
    rhs = assemble(running)

    def weighted(first_vec, second_vec):
        return jnp.sum(first_vec * second_vec * inv_mult)

    def squares(residual):
        return lax.psum(weighted(residual, residual), ("stream", "span"))

    pressure = jnp.zeros_like(rhs)
    residual = rhs
    direction = rhs
    norm_now = squares(residual)
    for iteration in range(ITERS):
        applied = apply_operator(direction, weight3, metric, diffmat)
        step_len = norm_now / lax.psum(weighted(direction, applied), ("stream", "span"))
        pressure = pressure + step_len * direction
        residual = residual - step_len * applied
        norm_next = squares(residual)
        direction = residual + norm_next / norm_now * direction
        norm_now = norm_next
    return (pressure, residual)


def solution(mesh):
    return jax.shard_map(
        on_device,
        mesh=mesh,
        in_specs=(
            P(None, "stream", "span", None),
            P("stream", "span", None),
            P(None, ("stream", "span")),
            P(None, ("stream", "span")),
            P(("stream", "span")),
            P(),
            P(("stream", "span"), None),
            P(("stream", "span")),
        ),
        out_specs=(P("stream", "span", None), P("stream", "span", None)),
        check_vma=False,
    )
```

profile of v0, /device:TPU:1, one launch (start us, length us, event | category | flops | bytes accessed | tf_op | source)
XLA Modules:
  0.0 554.8 jit_solution(15528119805396378433)
XLA Ops:
  7.8 8.6 %all-to-all-start = ((f32[32,8,8]{1,2,0:T(8,128)}), f32[32,8,8]{1,2,0:T(8,128)S(1)}, u32[]{:S(2)}, u32[]{:S(2)}) async-start(f32[32,8,8]{1,2,0:T(8,128)} %copy.228), calls=%async_computation | async-start | bytes 262144 | tf_op jit(solution)/shard_map/all_to_all | solution.py:177
  20.2 3.7 all-to-all-done
  25.5 4.6 copy.230
  30.0 6.9 %squeeze.15 = f32[1,8,16,1024]{3,2,1,0:T(8,128)S(1)} reshape(f32[1,1,8,2,8,128,8]{6,5,4,3,2,1,0:T(8,128)} %copy.230) | data formatting | bytes 1048576 | tf_op jit(solution)/shard_map/squeeze | solution.py:209
  36.9 4.6 copy.234
  41.5 6.9 %squeeze.18 = f32[1,8,16,1024]{3,2,1,0:T(8,128)S(1)} reshape(f32[1,1,8,2,8,128,8]{6,5,4,3,2,1,0:T(8,128)} %copy.234) | data formatting | bytes 1048576 | tf_op jit(solution)/shard_map/squeeze | solution.py:211
  49.8 4.6 copy.232
  54.4 6.9 %squeeze.17 = f32[8,2,8,1024]{3,2,1,0:T(8,128)S(1)} reshape(f32[1,1,8,2,8,128,8]{6,5,4,3,2,1,0:T(8,128)} %copy.232) | data formatting | bytes 1048576 | tf_op jit(solution)/shard_map/squeeze | solution.py:210
  65.2 3.5 collective-permute-start
  70.1 3.9 collective-permute-done.1
  74.2 3.8 collective-permute-start.2
  78.0 2.4 collective-permute-start.3
  81.0 2.2 collective-permute-done.3
  89.6 3.5 collective-permute-start.4
  94.5 4.9 collective-permute-done.5
  99.7 3.3 collective-permute-start.6
  103.0 1.9 collective-permute-start.7
  105.0 3.3 collective-permute-done.7
  109.6 80.7 %all-reduce.8 = (f32[]{:T(128)}, f32[]{:T(128)}) all-reduce(f32[]{:T(128)} %get-tuple-element.15, f32[]{:T(128)} %get-tuple-element.14), channel_id=1, replica_groups=mesh['stream'=8,'span'=32] {'stream','span'}, use_global_device_ids=true, to_apply=%region_5.6 | all-reduce | flops 2 | bytes 16 | tf_op jit(solution)/shard_map/psum | solution.py:218
  192.6 73.5 %psum.44 = f32[]{:T(128)} all-reduce(f32[]{:T(128)} %fusion.47), channel_id=1, replica_groups=mesh['stream'=8,'span'=32] {'stream','span'}, use_global_device_ids=true, to_apply=%region_9.10 | all-reduce | flops 1 | bytes 8 | tf_op jit(solution)/shard_map/psum | solution.py:218
  273.6 3.7 collective-permute-start.8
  278.6 3.7 collective-permute-done.9
  282.5 4.9 collective-permute-start.10
  287.5 1.9 collective-permute-start.11
  289.4 3.3 collective-permute-done.11
  293.9 76.7 %psum.45 = f32[]{:T(128)} all-reduce(f32[]{:T(128)} %get-tuple-element.22), channel_id=1, replica_groups=mesh['stream'=8,'span'=32] {'stream','span'}, use_global_device_ids=true, to_apply=%region_11.12 | all-reduce | flops 1 | bytes 8 | tf_op jit(solution)/shard_map/psum | solution.py:226
  372.9 73.5 %psum.46 = f32[]{:T(128)} all-reduce(f32[]{:T(128)} %get-tuple-element.20), channel_id=1, replica_groups=mesh['stream'=8,'span'=32] {'stream','span'}, use_global_device_ids=true, to_apply=%region_13.14 | all-reduce | flops 1 | bytes 8 | tf_op jit(solution)/shard_map/psum | solution.py:218
  453.6 3.7 collective-permute-start.12
  458.6 3.7 collective-permute-done.13
  462.6 5.0 collective-permute-start.14
  469.5 3.3 collective-permute-done.15
  473.9 76.7 %psum.47 = f32[]{:T(128)} all-reduce(f32[]{:T(128)} %get-tuple-element.18), channel_id=1, replica_groups=mesh['stream'=8,'span'=32] {'stream','span'}, use_global_device_ids=true, to_apply=%region_15.16 | all-reduce | flops 1 | bytes 8 | tf_op jit(solution)/shard_map/psum | solution.py:226
  (123 shorter events, 52.8 us)
Async XLA Ops:
  1.3 18.3 %copy-start.3 = (f32[8]{0:T(128)S(1)}, f32[8]{0:T(128)}, u32[]{:S(2)}) copy-start(f32[8]{0:T(128)} %constant.131.clone) | copy-start | bytes 100
  7.8 16.2 %all-to-all-start = ((f32[32,8,8]{1,2,0:T(8,128)}), f32[32,8,8]{1,2,0:T(8,128)S(1)}, u32[]{:S(2)}, u32[]{:S(2)}) async-start(f32[32,8,8]{1,2,0:T(8,128)} %copy.228), calls=%async_computation | async-start | bytes 262144 | tf_op jit(solution)/shard_map/all_to_all | solution.py:177
  18.7 5.4 copy-start.4
  54.4 6.9 %copy-start.2 = (f32[8,8,1,1]{0,1,3,2:T(8,128)S(1)}, f32[8,8,1,1]{0,1,3,2:T(8,128)}, u32[]{:S(2)}) copy-start(f32[8,8,1,1]{0,1,3,2:T(8,128)} %constant.158) | copy-start | bytes 772
  61.3 2.9 copy-start.1
  65.2 4.9 collective-permute-start
  68.8 5.2 collective-permute-start.1
  74.2 6.8 %collective-permute-start.2 = (f32[8,1,1024]{2,0,1:T(8,128)S(1)}, f32[8,1,1024]{2,0,1:T(8,128)S(1)}, u32[]{:S(2)}, u32[]{:S(2)}) collective-permute-start(f32[8,1,1024]{2,0,1:T(8,128)S(1)} %get-tuple-element.42), channel_id=1, source_target_pairs={{0,1},{1,2},{2,3},{3,4},{4,5},{5,6},{6,7},{7,8},{8,9},{9,10},{10,1... | collective-permute-start | bytes 98312 | tf_op jit(solution)/shard_map/ppermute | solution.py:28
  78.0 5.2 collective-permute-start.3
  83.4 1.6 copy-start
  89.6 4.9 collective-permute-start.4
  93.1 6.3 %collective-permute-start.5 = (f32[1,16,1024]{2,0,1:T(1,128)S(1)}, f32[1,16,1024]{2,0,1:T(1,128)S(1)}, u32[]{:S(2)}, u32[]{:S(2)}) collective-permute-start(f32[1,16,1024]{2,0,1:T(1,128)S(1)} %get-tuple-element.41), channel_id=1, source_target_pairs={{32,0},{64,32},{96,64},{128,96},{160,128},{192,160},{224,192},{33,... | collective-permute-start | bytes 196616 | tf_op jit(solution)/shard_map/ppermute | solution.py:29
  99.7 5.3 collective-permute-start.6
  103.0 5.2 collective-permute-start.7
  273.6 5.0 collective-permute-start.8
  277.3 5.0 collective-permute-start.9
  282.5 6.9 %collective-permute-start.10 = (f32[8,1,1024]{2,0,1:T(8,128)S(1)}, f32[8,1,1024]{2,0,1:T(8,128)S(1)}, u32[]{:S(2)}, u32[]{:S(2)}) collective-permute-start(f32[8,1,1024]{2,0,1:T(8,128)S(1)} %get-tuple-element.34), channel_id=1, source_target_pairs={{0,1},{1,2},{2,3},{3,4},{4,5},{5,6},{6,7},{7,8},{8,9},{9,10},{10,1... | collective-permute-start | bytes 98312 | tf_op jit(solution)/shard_map/ppermute | solution.py:28
  287.5 5.2 collective-permute-start.11
  453.6 5.0 collective-permute-start.12
  457.3 5.0 collective-permute-start.13
  462.6 6.9 %collective-permute-start.14 = (f32[8,1,1024]{2,0,1:T(8,128)S(1)}, f32[8,1,1024]{2,0,1:T(8,128)S(1)}, u32[]{:S(2)}, u32[]{:S(2)}) collective-permute-start(f32[8,1,1024]{2,0,1:T(8,128)S(1)} %get-tuple-element.30), channel_id=1, source_target_pairs={{0,1},{1,2},{2,3},{3,4},{4,5},{5,6},{6,7},{7,8},{8,9},{9,10},{10,1... | collective-permute-start | bytes 98312 | tf_op jit(solution)/shard_map/ppermute | solution.py:28
  467.5 5.2 collective-permute-start.15
where the time goes:
time: 565 us; the launch traced here: 555 us
  blocking collectives  381 us (67%)
  starting transfers between devices  53.3 us (9%)
  local copies, waits for them, and re-layouts  43.2 us (8%)
  waiting for transfers between devices  32.1 us (6%)
  other arithmetic  18.4 us (3%)
  matrix products  18.4 us (3%)
  between operations  8.33 us (1%)
    psum x3, blocking collectives, squares(): return lax.psum(weighted(residual, residual), ('stream', 'span'))  228 us
    psum x2, blocking collectives, on_device(): lax.psum(weighted(direction, applied), ('stream', 'span'))  153 us
    ppermute x8, starting transfers between devices, with_halo(): before = lax.ppermute(last, axis, up)  31.4 us
    ppermute x8, waiting for transfers between devices, with_halo(): after = lax.ppermute(first, axis, down)  28.3 us
    ppermute x8, starting transfers between devices, with_halo(): after = lax.ppermute(first, axis, down)  13.3 us
  transfers between devices with their start and end apart: 17, of which 9 were waited for; matrix products, arithmetic and copies ran while one was open for 1% of the time, Pallas kernels for 0%

commit v1 on v0

--- a/solution.py
+++ b/solution.py
@@ -215,7 +215,7 @@
         return jnp.sum(first_vec * second_vec * inv_mult)
 
     def squares(residual):
-        return lax.psum(weighted(residual, residual), ("stream", "span"))
+        return jnp.sum(lax.all_gather(weighted(residual, residual), ("stream", "span")), axis=0)
 
     pressure = jnp.zeros_like(rhs)
     residual = rhs

time: 565 us -> 569 us (level)
    psum x3 -> x0, blocking collectives: 228 us -> none  [squares(): return lax.psum(weighted(residual, residual), ('stream', 'span'))]
    unnamed x0 -> x3, blocking collectives: none -> 228 us
where the time goes in v1:
time: 569 us; the launch traced here: 559 us
  blocking collectives  381 us (67%)
  starting transfers between devices  53.4 us (9%)
  local copies, waits for them, and re-layouts  45.5 us (8%)
  waiting for transfers between devices  32.1 us (6%)
  other arithmetic  20.2 us (4%)
  matrix products  18.4 us (3%)
  between operations  8.35 us (1%)
    unnamed x3, blocking collectives  228 us
    psum x2, blocking collectives, on_device(): lax.psum(weighted(direction, applied), ('stream', 'span'))  153 us
    ppermute x8, starting transfers between devices, with_halo(): before = lax.ppermute(last, axis, up)  31.5 us
    ppermute x8, waiting for transfers between devices, with_halo(): after = lax.ppermute(first, axis, down)  28.3 us
    ppermute x8, starting transfers between devices, with_halo(): after = lax.ppermute(first, axis, down)  13.3 us
  transfers between devices with their start and end apart: 17, of which 9 were waited for; matrix products, arithmetic and copies ran while one was open for 1% of the time, Pallas kernels for 0%

profile of v1, /device:TPU:1, one launch (start us, length us, event | category | flops | bytes accessed | tf_op | source)
XLA Modules:
  0.0 559.0 jit_solution(7259559487240628648)
XLA Ops:
  7.8 8.6 %all-to-all-start = ((f32[32,8,8]{1,2,0:T(8,128)}), f32[32,8,8]{1,2,0:T(8,128)S(1)}, u32[]{:S(2)}, u32[]{:S(2)}) async-start(f32[32,8,8]{1,2,0:T(8,128)} %copy.228), calls=%async_computation | async-start | bytes 262144 | tf_op jit(solution)/shard_map/all_to_all | solution.py:177
  20.2 3.7 all-to-all-done
  25.4 4.6 copy.230
  30.0 6.9 %squeeze.15 = f32[1,8,16,1024]{3,2,1,0:T(8,128)S(1)} reshape(f32[1,1,8,2,8,128,8]{6,5,4,3,2,1,0:T(8,128)} %copy.230) | data formatting | bytes 1048576 | tf_op jit(solution)/shard_map/squeeze | solution.py:209
  36.9 4.6 copy.234
  41.5 6.9 %squeeze.18 = f32[1,8,16,1024]{3,2,1,0:T(8,128)S(1)} reshape(f32[1,1,8,2,8,128,8]{6,5,4,3,2,1,0:T(8,128)} %copy.234) | data formatting | bytes 1048576 | tf_op jit(solution)/shard_map/squeeze | solution.py:211
  49.8 4.6 copy.232
  54.4 6.9 %squeeze.17 = f32[8,2,8,1024]{3,2,1,0:T(8,128)S(1)} reshape(f32[1,1,8,2,8,128,8]{6,5,4,3,2,1,0:T(8,128)} %copy.232) | data formatting | bytes 1048576 | tf_op jit(solution)/shard_map/squeeze | solution.py:210
  65.2 3.5 collective-permute-start
  70.1 3.9 collective-permute-done.1
  74.3 3.8 collective-permute-start.2
  78.0 2.4 collective-permute-start.3
  81.0 2.3 collective-permute-done.3
  89.6 3.6 collective-permute-start.4
  94.5 4.9 collective-permute-done.5
  99.7 3.3 collective-permute-start.6
  105.0 3.3 collective-permute-done.7
  110.5 80.6 %all-reduce.11 = (f32[256]{0:T(256)S(1)}, f32[]{:T(128)}) all-reduce(f32[256]{0:T(256)S(1)} %dynamic-update-slice, f32[]{:T(128)} %get-tuple-element.14), channel_id=1, replica_groups=mesh['stream'=8,'span'=32] {'stream','span'}, use_global_device_ids=true, to_apply=%add.8 | all-reduce | flops 257 | bytes 2056
  194.8 73.5 %all-reduce.9 = f32[256]{0:T(256)S(1)} all-reduce(f32[256]{0:T(256)S(1)} %dynamic-update-slice.1), channel_id=1, replica_groups=mesh['stream'=8,'span'=32] {'stream','span'}, use_global_device_ids=true, to_apply=%add.9 | all-reduce | flops 256 | bytes 2048
  276.3 3.7 collective-permute-start.8
  281.3 3.7 collective-permute-done.9
  285.3 5.0 collective-permute-start.10
  290.3 1.9 collective-permute-start.11
  292.2 3.3 collective-permute-done.11
  296.7 76.7 %psum.22 = f32[]{:T(128)} all-reduce(f32[]{:T(128)} %get-tuple-element.22), channel_id=1, replica_groups=mesh['stream'=8,'span'=32] {'stream','span'}, use_global_device_ids=true, to_apply=%region_11.12 | all-reduce | flops 1 | bytes 8 | tf_op jit(solution)/shard_map/psum | solution.py:226
  376.4 73.5 %all-reduce.10 = f32[256]{0:T(256)S(1)} all-reduce(f32[256]{0:T(256)S(1)} %dynamic-update-slice.2), channel_id=1, replica_groups=mesh['stream'=8,'span'=32] {'stream','span'}, use_global_device_ids=true, to_apply=%add.10 | all-reduce | flops 256 | bytes 2048
  457.7 3.7 collective-permute-start.12
  462.7 3.7 collective-permute-done.13
  466.7 5.0 collective-permute-start.14
  471.7 1.9 collective-permute-start.15
  473.7 3.3 collective-permute-done.15
  478.1 76.7 %psum.23 = f32[]{:T(128)} all-reduce(f32[]{:T(128)} %get-tuple-element.18), channel_id=1, replica_groups=mesh['stream'=8,'span'=32] {'stream','span'}, use_global_device_ids=true, to_apply=%region_15.16 | all-reduce | flops 1 | bytes 8 | tf_op jit(solution)/shard_map/psum | solution.py:226
  (132 shorter events, 56.9 us)
Async XLA Ops:
  1.3 18.3 %copy-start.3 = (f32[8]{0:T(128)S(1)}, f32[8]{0:T(128)}, u32[]{:S(2)}) copy-start(f32[8]{0:T(128)} %constant.131.clone) | copy-start | bytes 100
  7.8 16.2 %all-to-all-start = ((f32[32,8,8]{1,2,0:T(8,128)}), f32[32,8,8]{1,2,0:T(8,128)S(1)}, u32[]{:S(2)}, u32[]{:S(2)}) async-start(f32[32,8,8]{1,2,0:T(8,128)} %copy.228), calls=%async_computation | async-start | bytes 262144 | tf_op jit(solution)/shard_map/all_to_all | solution.py:177
  18.7 5.4 copy-start.4
  54.4 6.9 %copy-start.2 = (f32[8,8,1,1]{0,1,3,2:T(8,128)S(1)}, f32[8,8,1,1]{0,1,3,2:T(8,128)}, u32[]{:S(2)}) copy-start(f32[8,8,1,1]{0,1,3,2:T(8,128)} %constant.170) | copy-start | bytes 772
  61.3 2.9 copy-start.1
  65.2 4.9 collective-permute-start
  68.8 5.2 collective-permute-start.1
  74.3 6.8 %collective-permute-start.2 = (f32[8,1,1024]{2,0,1:T(8,128)S(1)}, f32[8,1,1024]{2,0,1:T(8,128)S(1)}, u32[]{:S(2)}, u32[]{:S(2)}) collective-permute-start(f32[8,1,1024]{2,0,1:T(8,128)S(1)} %get-tuple-element.42), channel_id=1, source_target_pairs={{0,1},{1,2},{2,3},{3,4},{4,5},{5,6},{6,7},{7,8},{8,9},{9,10},{10,1... | collective-permute-start | bytes 98312 | tf_op jit(solution)/shard_map/ppermute | solution.py:28
  78.0 5.2 collective-permute-start.3
  83.4 1.6 copy-start
  89.6 4.9 collective-permute-start.4
  93.2 6.3 %collective-permute-start.5 = (f32[1,16,1024]{2,0,1:T(1,128)S(1)}, f32[1,16,1024]{2,0,1:T(1,128)S(1)}, u32[]{:S(2)}, u32[]{:S(2)}) collective-permute-start(f32[1,16,1024]{2,0,1:T(1,128)S(1)} %get-tuple-element.41), channel_id=1, source_target_pairs={{32,0},{64,32},{96,64},{128,96},{160,128},{192,160},{224,192},{33,... | collective-permute-start | bytes 196616 | tf_op jit(solution)/shard_map/ppermute | solution.py:29
  99.7 5.3 collective-permute-start.6
  103.0 5.2 collective-permute-start.7
  276.3 5.0 collective-permute-start.8
  280.0 5.0 collective-permute-start.9
  285.3 6.9 %collective-permute-start.10 = (f32[8,1,1024]{2,0,1:T(8,128)S(1)}, f32[8,1,1024]{2,0,1:T(8,128)S(1)}, u32[]{:S(2)}, u32[]{:S(2)}) collective-permute-start(f32[8,1,1024]{2,0,1:T(8,128)S(1)} %get-tuple-element.34), channel_id=1, source_target_pairs={{0,1},{1,2},{2,3},{3,4},{4,5},{5,6},{6,7},{7,8},{8,9},{9,10},{10,1... | collective-permute-start | bytes 98312 | tf_op jit(solution)/shard_map/ppermute | solution.py:28
  290.3 5.2 collective-permute-start.11
  457.7 5.0 collective-permute-start.12
  461.4 5.0 collective-permute-start.13
  466.7 7.0 %collective-permute-start.14 = (f32[8,1,1024]{2,0,1:T(8,128)S(1)}, f32[8,1,1024]{2,0,1:T(8,128)S(1)}, u32[]{:S(2)}, u32[]{:S(2)}) collective-permute-start(f32[8,1,1024]{2,0,1:T(8,128)S(1)} %get-tuple-element.30), channel_id=1, source_target_pairs={{0,1},{1,2},{2,3},{3,4},{4,5},{5,6},{6,7},{7,8},{8,9},{9,10},{10,1... | collective-permute-start | bytes 98312 | tf_op jit(solution)/shard_map/ppermute | solution.py:28
  471.7 5.2 collective-permute-start.15
